TPU v7x, 32 devices: a whole 2x2x4 slice. The times are simulated.
32 devices in a mesh: grp: 2 (over x), gx: 16 (over z, y, core).
Axes of the slice: x: 2, y: 2, z: 4, core: 2. Of those that a mesh axis runs over, the one named last changes fastest.
Arguments:
- e_forward: float32 [3, 256, 32, 256], P(None, ('grp', 'gx')), parts along dimension 1, may hold values from -6 to 6
- h_forward: float32 [3, 256, 32, 256], P(None, ('grp', 'gx')), parts along dimension 1, may hold values from -6 to 6
- p_forward: float32 [3, 256, 32, 256], P(None, ('grp', 'gx')), parts along dimension 1, may hold values from -6 to 6
- j_forward: float32 [3, 256, 32, 256], P(None, ('grp', 'gx')), parts along dimension 1, may hold values from -6 to 6
- e_adjoint: float32 [3, 256, 32, 256], P(None, ('grp', 'gx')), parts along dimension 1, may hold values from -6 to 6
- h_adjoint: float32 [3, 256, 32, 256], P(None, ('grp', 'gx')), parts along dimension 1, may hold values from -6 to 6
- p_adjoint: float32 [3, 256, 32, 256], P(None, ('grp', 'gx')), parts along dimension 1, may hold values from -6 to 6
- j_adjoint: float32 [3, 256, 32, 256], P(None, ('grp', 'gx')), parts along dimension 1, may hold values from -6 to 6
- design: float32 [32, 32, 256], P(('grp', 'gx')), parts along dimension 0, may hold values from 0 to 1
- source_amp: float32 [32, 3], P('grp'), parts along dimension 0, may hold values from -6 to 6
- source_cell: int32 [32], P('grp'), parts along dimension 0, may hold values from 0 to 1048575
- monitor_cell: int32 [32], P('grp'), parts along dimension 0, may hold values from 0 to 1048575
- slab_start: int32 [2], P('grp'), parts along dimension 0, may hold values from 8 to 15
- radius: int32 [2], P('grp'), parts along dimension 0, may hold values from 1 to 4
Outputs:
- e_forward_next: float32 [3, 256, 32, 256], P(None, ('grp', 'gx')), parts along dimension 1
- h_forward_next: float32 [3, 256, 32, 256], P(None, ('grp', 'gx')), parts along dimension 1
- e_adjoint_next: float32 [3, 256, 32, 256], P(None, ('grp', 'gx')), parts along dimension 1
- h_adjoint_next: float32 [3, 256, 32, 256], P(None, ('grp', 'gx')), parts along dimension 1
- design_grad: float32 [32, 32, 256], P(('grp', 'gx')), parts along dimension 0
There are 2 independent parts, one for each index of `grp`. A program takes and returns all parts, laid end to end along the dimension named above; each array names one. Nothing has to cross between parts.
Inputs may be any that keep to these rules, and one draw needn't show every extreme that they name: `slab_start`: the slab begins within planes 8 to 15 of the grid.
All inputs are finite; a program needn't handle non-finite values.
Results may differ from a plain program's by a relative error of at most 0.0003.
Values sent between devices are 32-bit elements; how exact they have to be, the bound alone decides.
No kernel may reach another device: no remote copies, remote signals or barrier semaphores. Data moves between devices by JAX's collectives and lax.ppermute only.
A program may use at most 128 MiB of HBM per device.

v0:
```python
import jax
import jax.numpy as jnp
from jax import lax
from jax.sharding import PartitionSpec as P

DT = 0.5
EPS_RANGE = 10.0
STRENGTH_BASE = 0.5
STRENGTH_RANGE = 3.0
DAMPING = 0.2
GAIN_FIELD = 0.25
HIGH = lax.Precision.HIGHEST


def passed_along(block, axis, distance):
    devices = range(lax.axis_size(axis))
    route = [(i - distance, i) for i in devices if i - distance in devices]
    return lax.ppermute(block, axis, route)


def band_matrix(count, radius):
    rows = jnp.arange(count, dtype=jnp.int32)
    dist = jnp.abs(rows[:, None] - rows[None, :])
    weights = jnp.maximum(radius + 1 - dist, 0).astype(jnp.float32)
    return weights / jnp.sum(weights, axis=1, keepdims=True)


def ahead(field, axis):
    count = field.shape[axis]
    rest = lax.slice_in_dim(field, 1, count, axis=axis)
    return jnp.concatenate([rest, jnp.zeros_like(lax.slice_in_dim(field, 0, 1, axis=axis))], axis)


def behind(field, axis):
    count = field.shape[axis]
    rest = lax.slice_in_dim(field, 0, count - 1, axis=axis)
    return jnp.concatenate([jnp.zeros_like(lax.slice_in_dim(field, 0, 1, axis=axis)), rest], axis)


def update_h(efield, hfield, upper):
    ex, ey, ez = (efield[0], efield[1], efield[2])
    ex_next = jnp.concatenate([ex[1:], upper[0][None]], 0)
    ey_next = jnp.concatenate([ey[1:], upper[1][None]], 0)
    curl_x = ahead(ez, 2) - ez - (ey_next - ey)
    curl_y = ex_next - ex - (ahead(ez, 1) - ez)
    curl_z = ahead(ey, 1) - ey - (ahead(ex, 2) - ex)
    return hfield - DT * jnp.stack([curl_x, curl_y, curl_z])


def update_e(efield, hnext, lower, jnext, permittivity, drive):
    hx, hy, hz = (hnext[0], hnext[1], hnext[2])
    hx_prev = jnp.concatenate([lower[0][None], hx[:-1]], 0)
    hy_prev = jnp.concatenate([lower[1][None], hy[:-1]], 0)
    curl_x = hz - behind(hz, 2) - (hy - hy_prev)
    curl_y = hx - hx_prev - (hz - behind(hz, 1))
    curl_z = hy - behind(hy, 1) - (hx - behind(hx, 2))
    curl = jnp.stack([curl_x, curl_y, curl_z])
    return efield + (DT / permittivity)[None] * (curl - jnext + drive)


def update_j(jfield, pfield, efield, strength):
    return ((1.0 - DAMPING * DT / 2.0) * jfield + DT * (strength[None] * efield - pfield)) / (
        1.0 + DAMPING * DT / 2.0
    )


def smooth(wx, wy, planes):
    inner = jnp.einsum("ax,zxy->zay", wx, planes, precision=HIGH)
    return jnp.einsum("zay,by->zab", inner, wy, precision=HIGH)


def smooth_adjoint(wx, wy, planes):
    inner = jnp.einsum("ax,zab->zxb", wx, planes, precision=HIGH)
    return jnp.einsum("zxb,by->zxy", inner, wy, precision=HIGH)


def locate(cells, first, depth, width_x, width_y):
    zz = cells // (width_x * width_y)
    rest = cells % (width_x * width_y)
    local = zz - first
    inside = ((local >= 0) & (local < depth)).astype(jnp.float32)
    return (jnp.clip(local, 0, depth - 1), rest // width_y, rest % width_y, inside)


def body(
    e_forward,
    h_forward,
    p_forward,
    j_forward,
    e_adjoint,
    h_adjoint,
    p_adjoint,
    j_adjoint,
    design,
    source_amp,
    source_cell,
    monitor_cell,
    slab_start,
    radius,
):
    index = lax.axis_index("gx")
    depth, width_x, width_y = (e_forward.shape[1], e_forward.shape[2], e_forward.shape[3])
    start = slab_start[0]
    wx = band_matrix(width_x, radius[0])
    wy = band_matrix(width_y, radius[0])
    upper = passed_along(
        jnp.stack([e_forward[0, 0], e_forward[1, 0], e_adjoint[0, 0], e_adjoint[1, 0]]), "gx", -1
    )
    hf = update_h(e_forward, h_forward, upper[0:2])
    ha = update_h(e_adjoint, h_adjoint, upper[2:4])
    gathered = lax.all_gather(design, "gx", axis=0, tiled=True)
    slab = gathered.shape[0]
    planes = index * depth + jnp.arange(depth, dtype=jnp.int32) - start
    valid = ((planes >= 0) & (planes < slab)).astype(jnp.float32)
    picked = jnp.take(gathered, jnp.clip(planes, 0, slab - 1), axis=0) * valid[:, None, None]
    density = smooth(wx, wy, picked)
    permittivity = 1.0 + EPS_RANGE * density
    strength = STRENGTH_BASE + STRENGTH_RANGE * density
    lower = passed_along(jnp.stack([hf[0, -1], hf[1, -1], ha[0, -1], ha[1, -1]]), "gx", 1)
    zs, xs, ys, inside_s = locate(source_cell, index * depth, depth, width_x, width_y)
    nsrc = zs.shape[0]
    comp = jnp.repeat(jnp.arange(3, dtype=jnp.int32), nsrc)
    drive = (
        jnp.zeros((3, depth, width_x, width_y), jnp.float32)
        .at[comp, jnp.tile(zs, 3), jnp.tile(xs, 3), jnp.tile(ys, 3)]
        .add((source_amp.T * inside_s[None, :]).reshape(-1))
    )
    zm, xm, ym, inside_m = locate(monitor_cell, index * depth, depth, width_x, width_y)
    count = jnp.zeros((depth, width_x, width_y), jnp.float32).at[zm, xm, ym].add(inside_m)
    drive_adj = count[None] * e_forward
    jf = update_j(j_forward, p_forward, e_forward, strength)
    ja = update_j(j_adjoint, p_adjoint, e_adjoint, strength)
    ef = update_e(e_forward, hf, lower[0:2], jf, permittivity, drive)
    ea = update_e(e_adjoint, ha, lower[2:4], ja, permittivity, drive_adj)
    intersection = jnp.sum(ea * (ef - e_forward + GAIN_FIELD * ef), axis=0)
    slots = jnp.arange(slab, dtype=jnp.int32)
    select = (planes[:, None] == slots[None, :]).astype(jnp.float32)
    returned = jnp.einsum("lo,lxy->oxy", select, intersection, precision=HIGH)
    own_intersection = lax.psum_scatter(returned, "gx", scatter_dimension=0, tiled=True)
    design_grad = smooth_adjoint(wx, wy, own_intersection)
    return (ef, hf, ea, ha, design_grad)


def solution(mesh):
    return jax.shard_map(
        body,
        mesh=mesh,
        in_specs=(
            P(None, ("grp", "gx"), None, None),
            P(None, ("grp", "gx"), None, None),
            P(None, ("grp", "gx"), None, None),
            P(None, ("grp", "gx"), None, None),
            P(None, ("grp", "gx"), None, None),
            P(None, ("grp", "gx"), None, None),
            P(None, ("grp", "gx"), None, None),
            P(None, ("grp", "gx"), None, None),
            P(("grp", "gx"), None, None),
            P("grp", None),
            P("grp"),
            P("grp"),
            P("grp"),
            P("grp"),
        ),
        out_specs=(
            P(None, ("grp", "gx"), None, None),
            P(None, ("grp", "gx"), None, None),
            P(None, ("grp", "gx"), None, None),
            P(None, ("grp", "gx"), None, None),
            P(("grp", "gx"), None, None),
        ),
        check_vma=False,
    )
```

profile of v0, /device:TPU:0, one launch (start us, length us, event | category | flops | bytes accessed | tf_op | source)
XLA Modules:
  0.0 142.5 jit_solution(9310592674110908171)
XLA Ops:
  7.2 0.9 slice_bitcast_fusion.25
  8.1 0.7 pad_maximum_fusion
  8.8 1.3 collective-permute-start
  10.7 0.7 convert_reduce_fusion.1
  11.4 0.7 convert_reduce_fusion
  12.1 1.9 %slice_bitcast_fusion.17 = (f32[7,32,256]{2,1,0:T(8,128)}, f32[7,32,256]{2,1,0:T(8,128)}) fusion(f32[3,8,32,256]{3,2,1,0:T(8,128)} %param.18), kind=kLoop, calls=%fused_computation.73 | loop fusion | bytes 917504 | tf_op jit(solution)/shard_map/slice | solution.py:43
  14.0 0.8 slice_bitcast_fusion.19
  15.0 0.8 slice_bitcast_fusion.11
  15.8 0.7 slice.272
  16.6 0.8 slice.269
  18.1 0.5 compare_and_fusion
  18.6 0.6 copy-done.28
  19.2 0.5 and_convert_fusion.2
  19.7 0.7 reshape.193
  20.5 0.6 tile.32
  21.1 0.6 tile.30
  21.7 0.6 tile.13
  22.5 25.4 %all_gather.3 = f32[16,32,256]{2,1,0:T(8,128)S(1)} all-gather(f32[1,32,256]{2,1,0:T(8,128)} %param.22), channel_id=1, replica_groups=mesh['grp'=2,'gx'=16] {'gx'}, dimensions={0}, use_global_device_ids=true | all-gather | bytes 557056 | tf_op jit(solution)/shard_map/all_gather | solution.py:111
  47.9 0.7 slice.284
  48.7 0.8 copy-done.11
  49.6 0.8 slice.274
  50.4 0.7 slice.273
  51.1 0.6 gather_fusion
  51.7 0.6 copy-done.30
  52.4 0.4 convolution_bitcast_fusion
  53.1 1.3 add_divide_fusion
  54.5 1.6 %scatter_fusion.1 = f32[8,32,256]{2,1,0:T(8,128)S(1)} fusion(f32[8,32,256]{2,1,0:T(8,128)S(1)} %broadcast_in_dim.23, s32[16]{0:T(128)S(1)} %fusion.56, f32[16]{0:T(128)S(1)} %get-tuple-element.8), kind=kCustom, calls=%fused_computation.2 | custom fusion | flops 16 | bytes 384 | tf_op jit(solution)/shard_map/scatter-add | solution.py:129
  56.1 0.9 copy-done.10
  57.2 0.9 copy-done.20
  58.3 0.9 slice_bitcast_fusion.13
  59.2 0.9 slice_bitcast_fusion.2
  60.2 0.3 copy-done.7
  61.0 0.9 copy-done.21
  62.2 2.3 %collective-permute-start.1 = (f32[4,32,256]{2,1,0:T(8,128)S(1)}, f32[4,32,256]{2,1,0:T(8,128)S(1)}, u32[]{:S(2)}, u32[]{:S(2)}) collective-permute-start(f32[4,32,256]{2,1,0:T(8,128)S(1)} %pad_maximum_fusion.1), channel_id=1, source_target_pairs={{0,1},{1,2},{2,3},{3,4},{4,5},{5,6},{6,7},{7,8},{8,9},{9,10},{10,1... | collective-permute-start | bytes 393224 | tf_op jit(solution)/shard_map/ppermute | solution.py:18
  64.5 0.9 collective-permute-done.1
  65.5 0.4 fusion.14
  65.8 0.6 copy-done.4
  66.4 0.3 copy-done.16
  66.9 0.3 maximum_subtract_fusion
  67.3 4.2 %scatter_fusion = f32[3,8,32,256]{3,2,1,0:T(8,128)S(1)} fusion(f32[3,8,32,256]{3,2,1,0:T(8,128)S(1)} %maximum_subtract_fusion, s32[48]{0:T(128)S(1)} %fusion.59, f32[48]{0:T(128)S(1)} %reshape.207), kind=kCustom, calls=%fused_computation.1 | custom fusion | flops 48 | bytes 1344 | tf_op jit(solution)/shard_map/scatter-add | solution.py:126
  71.5 1.7 %fusion.18 = (f32[1,8,32,256]{3,2,1,0:T(8,128)S(1)}, f32[1,8,32,256]{3,2,1,0:T(8,128)S(1)}, f32[1,8,32,256]{3,2,1,0:T(8,128)S(1)}) fusion(f32[7,32,256]{2,1,0:T(8,128)} %get-tuple-element.28, f32[1,32,256]{2,1,0:T(8,128)S(1)} %get-tuple-element.61, f32[8,32,255]{2,1,0:T(8,128)} %bitcast.192, f32[3,8,32,256]{3,2,1,0:T(8,128)S(1)} %fusion.1, ...), kind=kLoop, calls=%fused_computation.43 | loop fusion | flops 720896 | bytes 3127296 | tf_op jit(solution)/shard_map/stack | solution.py:57
  73.5 1.8 %multiply_reduce_fusion = (f32[8,32,256]{2,1,0:T(8,128)S(1)}, f32[3,8,32,256]{3,2,1,0:T(8,128)}, f32[3,8,32,256]{3,2,1,0:T(8,128)}) fusion(f32[3,8,32,256]{3,2,1,0:T(8,128)S(1)} %copy-done, f32[3,8,32,256]{3,2,1,0:T(8,128)S(1)} %copy-done.1, f32[8,32,256]{2,1,0:T(8,128)S(1)} %scatter_fusion.1, f32[3,8,32,256]{3,2,1,0:T(8,128)S(1)} %copy-done.18, ...), kind=kLoop, calls=%fused_computation.15 | loop fusion | flops 3866624 | bytes 7340032 | tf_op jit(solution)/shard_map/reduce_sum | solution.py:135
  75.3 0.7 copy-done.29
  76.0 0.5 fusion.23
  76.5 1.1 copy.22
  77.7 55.9 %reduce-scatter.2.cloned.1.call-done = f32[1,32,256]{2,1,0:T(8,128)} async-done(((f32[16,32,256]{2,1,0:T(8,128)}), f32[1,32,256]{2,1,0:T(8,128)}) %reduce-scatter.2.cloned.1.call-update) | async-done | bytes 32784 | tf_op jit(solution)/shard_map/reduce_scatter | solution.py:139
  133.6 1.0 convolution_bitcast_fusion.2
  134.7 0.9 convolution_bitcast_fusion.1
  (99 shorter events, 2.7 us)
Async XLA Ops:
  7.2 6.9 %copy-start = (f32[3,8,32,256]{3,2,1,0:T(8,128)S(1)}, f32[3,8,32,256]{3,2,1,0:T(8,128)}, u32[]{:S(2)}) copy-start(f32[3,8,32,256]{3,2,1,0:T(8,128)} %param.14) | copy-start | bytes 2359300
  7.2 126.4 %reduce-scatter.2.cloned.1.call-start = ((), (), s32[]{:S(2)}) async-start(), calls=%async_computation.1 | async-start | bytes 557056 | tf_op jit(solution)/shard_map/reduce_scatter | solution.py:139
  8.8 47.3 %collective-permute-start = (f32[4,32,256]{2,1,0:T(8,128)}, f32[4,32,256]{2,1,0:T(8,128)S(1)}, u32[]{:S(2)}, u32[]{:S(2)}) collective-permute-start(f32[4,32,256]{2,1,0:T(8,128)} %pad_maximum_fusion), channel_id=1, source_target_pairs={{1,0},{2,1},{3,2},{4,3},{5,4},{6,5},{7,6},{8,7},{9,8},{10,9},{11,1... | collective-permute-start | bytes 393224 | tf_op jit(solution)/shard_map/ppermute | solution.py:18
  12.1 2.7 %copy-start.1 = (f32[3,8,32,256]{3,2,1,0:T(8,128)S(1)}, f32[3,8,32,256]{3,2,1,0:T(8,128)}, u32[]{:S(2)}) copy-start(f32[3,8,32,256]{3,2,1,0:T(8,128)} %param.18) | copy-start | bytes 2359300
  18.6 0.6 copy-start.28
  19.7 0.7 copy-start.31
  19.7 0.7 copy-start.32
  21.7 0.7 copy-start.27
  48.6 0.9 copy-start.11
  51.7 0.7 copy-start.30
  51.7 0.6 copy-start.33
  51.7 0.7 copy-start.35
  52.4 0.7 copy-start.36
  54.4 1.6 %copy-start.23 = (s32[48,1]{0,1:T(1,128)S(1)}, s32[48,1]{0,1:T(1,128)}, u32[]{:S(2)}) copy-start(s32[48,1]{0,1:T(1,128)} %reshape.193) | copy-start | bytes 580
  54.4 1.6 %copy-start.24 = (s32[48,1]{0,1:T(1,128)S(1)}, s32[48,1]{0,1:T(1,128)}, u32[]{:S(2)}) copy-start(s32[48,1]{0,1:T(1,128)} %tile.32) | copy-start | bytes 580
  54.4 1.6 %copy-start.25 = (s32[48,1]{0,1:T(1,128)S(1)}, s32[48,1]{0,1:T(1,128)}, u32[]{:S(2)}) copy-start(s32[48,1]{0,1:T(1,128)} %tile.30) | copy-start | bytes 580
  54.4 1.6 %copy-start.26 = (s32[48,1]{0,1:T(1,128)S(1)}, s32[48,1]{0,1:T(1,128)}, u32[]{:S(2)}) copy-start(s32[48,1]{0,1:T(1,128)} %tile.13) | copy-start | bytes 580
  54.4 1.7 %copy-start.14 = (f32[7,32,256]{2,1,0:T(8,128)S(1)}, f32[7,32,256]{2,1,0:T(8,128)}, u32[]{:S(2)}) copy-start(f32[7,32,256]{2,1,0:T(8,128)} %get-tuple-element.48) | copy-start | bytes 688132
  54.4 1.7 %copy-start.15 = (f32[7,32,256]{2,1,0:T(8,128)S(1)}, f32[7,32,256]{2,1,0:T(8,128)}, u32[]{:S(2)}) copy-start(f32[7,32,256]{2,1,0:T(8,128)} %get-tuple-element.49) | copy-start | bytes 688132
  56.1 1.0 copy-start.10
  57.0 1.1 copy-start.20
  58.3 13.2 %copy-start.2 = (f32[3,8,32,256]{3,2,1,0:T(8,128)}, f32[3,8,32,256]{3,2,1,0:T(8,128)S(1)}, u32[]{:S(2)}) copy-start(f32[3,8,32,256]{3,2,1,0:T(8,128)S(1)} %fusion.1) | copy-start | bytes 2359300
  59.2 1.0 copy-start.6
  59.2 1.2 copy-start.7
  59.2 1.4 copy-start.8
  59.2 1.5 %copy-start.9 = (f32[8,31,256]{2,1,0:T(8,128)S(1)}, f32[8,31,256]{2,1,0:T(8,128)}, u32[]{:S(2)}) copy-start(f32[8,31,256]{2,1,0:T(8,128)} %slice.273) | copy-start | bytes 761860
  59.2 1.5 %copy-start.12 = (f32[7,32,256]{2,1,0:T(8,128)S(1)}, f32[7,32,256]{2,1,0:T(8,128)}, u32[]{:S(2)}) copy-start(f32[7,32,256]{2,1,0:T(8,128)} %get-tuple-element.38) | copy-start | bytes 688132
  59.2 1.6 %copy-start.13 = (f32[7,32,256]{2,1,0:T(8,128)S(1)}, f32[7,32,256]{2,1,0:T(8,128)}, u32[]{:S(2)}) copy-start(f32[7,32,256]{2,1,0:T(8,128)} %get-tuple-element.39) | copy-start | bytes 688132
  60.8 1.1 copy-start.21
  62.1 3.4 %copy-start.3 = (f32[3,8,32,256]{3,2,1,0:T(8,128)}, f32[3,8,32,256]{3,2,1,0:T(8,128)S(1)}, u32[]{:S(2)}) copy-start(f32[3,8,32,256]{3,2,1,0:T(8,128)S(1)} %fusion) | copy-start | bytes 2359300
  62.2 3.2 %collective-permute-start.1 = (f32[4,32,256]{2,1,0:T(8,128)S(1)}, f32[4,32,256]{2,1,0:T(8,128)S(1)}, u32[]{:S(2)}, u32[]{:S(2)}) collective-permute-start(f32[4,32,256]{2,1,0:T(8,128)S(1)} %pad_maximum_fusion.1), channel_id=1, source_target_pairs={{0,1},{1,2},{2,3},{3,4},{4,5},{5,6},{6,7},{7,8},{8,9},{9,10},{10,1... | collective-permute-start | bytes 393224 | tf_op jit(solution)/shard_map/ppermute | solution.py:18
  65.4 1.0 copy-start.4
  65.5 1.2 copy-start.16
  65.5 1.4 %copy-start.17 = (f32[3,8,32,256]{3,2,1,0:T(8,128)S(1)}, f32[3,8,32,256]{3,2,1,0:T(8,128)}, u32[]{:S(2)}) copy-start(f32[3,8,32,256]{3,2,1,0:T(8,128)} %param.17) | copy-start | bytes 2359300
  71.5 1.8 %copy-start.5 = (f32[8,32,256]{2,1,0:T(8,128)S(1)}, f32[8,32,256]{2,1,0:T(8,128)}, u32[]{:S(2)}) copy-start(f32[8,32,256]{2,1,0:T(8,128)} %get-tuple-element.58) | copy-start | bytes 786436
  71.5 1.8 %copy-start.18 = (f32[3,8,32,256]{3,2,1,0:T(8,128)S(1)}, f32[3,8,32,256]{3,2,1,0:T(8,128)}, u32[]{:S(2)}) copy-start(f32[3,8,32,256]{3,2,1,0:T(8,128)} %param.20) | copy-start | bytes 2359300
  71.5 1.9 %copy-start.19 = (f32[3,8,32,256]{3,2,1,0:T(8,128)S(1)}, f32[3,8,32,256]{3,2,1,0:T(8,128)}, u32[]{:S(2)}) copy-start(f32[3,8,32,256]{3,2,1,0:T(8,128)} %param.21) | copy-start | bytes 2359300
  71.5 2.0 %copy-start.22 = (f32[8,32,256]{2,1,0:T(8,128)S(1)}, f32[8,32,256]{2,1,0:T(8,128)}, u32[]{:S(2)}) copy-start(f32[8,32,256]{2,1,0:T(8,128)} %get-tuple-element.57) | copy-start | bytes 786436
  75.3 0.7 copy-start.29
  77.6 56.0 %copy-start.34 = (f32[32]{0:T(128)S(1)}, f32[32]{0:T(128)}, u32[]{:S(2)}) copy-start(f32[32]{0:T(128)} %convert_reduce_fusion.1) | copy-start | bytes 388
  77.6 57.0 %copy-start.37 = (f32[256]{0:T(256)S(1)}, f32[256]{0:T(256)}, u32[]{:S(2)}) copy-start(f32[256]{0:T(256)} %convert_reduce_fusion) | copy-start | bytes 3076
Sparse Core Ops, SparseCore 0:
  77.8 55.7 reduce-scatter.1
where the time goes:
time: 143 us; the launch traced here: 142 us
  waiting for transfers between devices  56.9 us (40%)
  blocking collectives  25.4 us (18%)
  local copies, waits for them, and re-layouts  22.6 us (16%)
  between operations  15.9 us (11%)
  other arithmetic  13.9 us (10%)
  matrix products  4.26 us (3%)
  starting transfers between devices  3.57 us (2%)
    reduce_scatter x1, waiting for transfers between devices, body(): lax.psum_scatter(returned, 'gx', scatter_dimension=0, tiled=True)  55.9 us
    all_gather x1, blocking collectives, body(): gathered = lax.all_gather(design, 'gx', axis=0, tiled=True)  25.4 us
    unnamed x76, local copies, waits for them, and re-layouts  7.77 us
    scatter-add x1, other arithmetic, body(): drive = jnp.zeros((3, depth, width_x, width_y), jnp.float32).at[comp, jnp...  4.22 us
    slice x8, local copies, waits for them, and re-layouts, ahead(): rest = lax.slice_in_dim(field, 1, count, axis=axis)  4.17 us
    ppermute x2, starting transfers between devices, passed_along(): return lax.ppermute(block, axis, route)  3.53 us
  transfers between devices with their start and end apart: 3, of which 2 were waited for; matrix products, arithmetic and copies ran while one was open for 12% of the time, Pallas kernels for 0%

commit v1 on v0

--- a/solution.py
+++ b/solution.py
@@ -108,7 +108,14 @@
     )
     hf = update_h(e_forward, h_forward, upper[0:2])
     ha = update_h(e_adjoint, h_adjoint, upper[2:4])
-    gathered = lax.all_gather(design, "gx", axis=0, tiled=True)
+    ways, here, step = (lax.axis_size("gx"), lax.axis_index("gx"), design.shape[0])
+    line, have = (design, 1)
+    while have < ways:
+        line = jnp.concatenate(
+            [line, lax.ppermute(line, "gx", [(d, (d - have) % ways) for d in range(ways)])], axis=0
+        )
+        have = 2 * have
+    gathered = jnp.roll(line, here * step, axis=0)
     slab = gathered.shape[0]
     planes = index * depth + jnp.arange(depth, dtype=jnp.int32) - start
     valid = ((planes >= 0) & (planes < slab)).astype(jnp.float32)

time: 143 us -> 134 us (0.937)
  blocking collectives: 25.4 us -> 0 us
  waiting for transfers between devices: 56.9 us -> 71.2 us
  starting transfers between devices: 3.57 us -> 10.4 us
  local copies, waits for them, and re-layouts: 22.6 us -> 17.3 us
    all_gather x1 -> x0, blocking collectives: 25.4 us -> none  [body(): gathered = lax.all_gather(design, 'gx', axis=0, tiled=True)]
    ppermute x0 -> x4, waiting for transfers between devices: none -> 15.2 us  [body(): lax.ppermute(line, 'gx', [(d, (d - have) % ways) for d in range(ways)])]
    ppermute x0 -> x4, starting transfers between devices: none -> 7.56 us  [body(): lax.ppermute(line, 'gx', [(d, (d - have) % ways) for d in range(ways)])]
    slice x8, local copies, waits for them, and re-layouts: 4.17 us -> 2.01 us  [ahead(): rest = lax.slice_in_dim(field, 1, count, axis=axis)]
    unnamed x76 -> x63, local copies, waits for them, and re-layouts: 7.77 us -> 7.65 us
  transfers between devices with their start and end apart: 3 -> 7, of which waited for: 2 -> 4; matrix products, arithmetic and copies ran while one was open for 12% -> 11% of each run, Pallas kernels for 0% -> 0%
where the time goes in v1:
time: 134 us; the launch traced here: 133 us
  waiting for transfers between devices  71.2 us (53%)
  local copies, waits for them, and re-layouts  17.3 us (13%)
  between operations  16 us (12%)
  other arithmetic  14.3 us (11%)
  starting transfers between devices  10.4 us (8%)
  matrix products  4.19 us (3%)
    reduce_scatter x1, waiting for transfers between devices, body(): lax.psum_scatter(returned, 'gx', scatter_dimension=0, tiled=True)  55.1 us
    ppermute x4, waiting for transfers between devices, body(): lax.ppermute(line, 'gx', [(d, (d - have) % ways) for d in range(ways)])  15.2 us
    unnamed x63, local copies, waits for them, and re-layouts  7.65 us
    ppermute x4, starting transfers between devices, body(): lax.ppermute(line, 'gx', [(d, (d - have) % ways) for d in range(ways)])  7.56 us
    scatter-add x1, other arithmetic, body(): drive = jnp.zeros((3, depth, width_x, width_y), jnp.float32).at[comp, jnp...  4.22 us
    reduce_sum x1, other arithmetic, body(): intersection = jnp.sum(ea * (ef - e_forward + GAIN_FIELD * ef), axis=0)  3.25 us
    ppermute x2, starting transfers between devices, passed_along(): return lax.ppermute(block, axis, route)  2.84 us
  transfers between devices with their start and end apart: 7, of which 4 were waited for; matrix products, arithmetic and copies ran while one was open for 11% of the time, Pallas kernels for 0%

profile of v1, /device:TPU:0, one launch (start us, length us, event | category | flops | bytes accessed | tf_op | source)
XLA Modules:
  0.0 133.4 jit_solution(16941229090689174029)
XLA Ops:
  7.2 0.8 slice_bitcast_fusion.25
  8.0 0.7 pad_maximum_fusion.2
  8.7 1.4 %collective-permute-start.4 = (f32[4,32,256]{2,1,0:T(8,128)}, f32[4,32,256]{2,1,0:T(8,128)}, u32[]{:S(2)}, u32[]{:S(2)}) collective-permute-start(f32[4,32,256]{2,1,0:T(8,128)} %pad_maximum_fusion.2), channel_id=1, source_target_pairs={{1,0},{2,1},{3,2},{4,3},{5,4},{6,5},{7,6},{8,7},{9,8},{10,9},{11,1... | collective-permute-start | bytes 393224 | tf_op jit(solution)/shard_map/ppermute | solution.py:18
  10.1 7.4 %collective-permute-start = (f32[1,32,256]{2,1,0:T(8,128)S(1)}, f32[1,32,256]{2,1,0:T(8,128)S(1)}, u32[]{:S(2)}, u32[]{:S(2)}) collective-permute-start(f32[1,32,256]{2,1,0:T(8,128)S(1)} %copy-done.18), channel_id=1, source_target_pairs={{0,15},{1,0},{2,1},{3,2},{4,3},{5,4},{6,5},{7,6},{8,7},{9,8},{10,9... | collective-permute-start | bytes 98312 | tf_op jit(solution)/shard_map/ppermute | solution.py:115
  17.5 1.2 slice_bitcast_fusion.11
  18.7 0.8 slice_bitcast_fusion.19
  19.5 0.5 copy-done.1
  20.0 0.8 slice_bitcast_fusion.8
  20.8 0.8 slice_bitcast_fusion.17
  21.6 0.6 constant_dynamic-update-slice_fusion.9
  22.9 0.6 copy-done.25
  24.0 0.7 copy-done.24
  24.7 0.1 slice.269
  24.9 0.1 slice.280
  25.1 0.7 slice.273
  25.8 0.8 slice.274
  26.8 0.9 copy-done.13
  27.7 0.1 slice.285
  28.6 1.6 %scatter_fusion.1 = f32[8,32,256]{2,1,0:T(8,128)S(1)} fusion(f32[8,32,256]{2,1,0:T(8,128)S(1)} %broadcast_in_dim.23, s32[16]{0:T(128)S(1)} %fusion.56, f32[16]{0:T(128)S(1)} %get-tuple-element.8), kind=kCustom, calls=%fused_computation.2 | custom fusion | flops 16 | bytes 384 | tf_op jit(solution)/shard_map/scatter-add | solution.py:136
  30.2 0.1 convert_reduce_fusion.1
  30.3 0.2 convert_reduce_fusion
  30.5 0.6 constant_dynamic-update-slice_fusion.8
  31.1 3.6 %collective-permute-done.1 = f32[2,32,256]{2,1,0:T(8,128)S(1)} collective-permute-done((f32[2,32,256]{2,1,0:T(8,128)S(1)}, f32[2,32,256]{2,1,0:T(8,128)S(1)}, u32[]{:S(2)}, u32[]{:S(2)}) %collective-permute-start.1) | collective-permute-done | bytes 65568 | tf_op jit(solution)/shard_map/ppermute | solution.py:115
  34.9 0.6 constant_dynamic-update-slice_fusion.7
  35.5 0.8 fusion.69
  36.4 1.2 fusion.6
  37.6 0.1 fusion
  37.9 1.1 copy-done.15
  39.1 0.2 fusion.10
  39.3 0.9 copy-done.22
  40.2 0.1 fusion.1
  40.4 1.4 %collective-permute-start.5 = (f32[4,32,256]{2,1,0:T(8,128)S(1)}, f32[4,32,256]{2,1,0:T(8,128)S(1)}, u32[]{:S(2)}, u32[]{:S(2)}) collective-permute-start(f32[4,32,256]{2,1,0:T(8,128)S(1)} %pad_maximum_fusion.3), channel_id=1, source_target_pairs={{0,1},{1,2},{2,3},{3,4},{4,5},{5,6},{6,7},{7,8},{8,9},{9,10},{10,1... | collective-permute-start | bytes 393224 | tf_op jit(solution)/shard_map/ppermute | solution.py:18
  42.1 0.8 collective-permute-done.5
  42.9 1.1 fusion.14
  44.0 1.1 fusion.18
  45.1 11.6 %collective-permute-done.3 = f32[8,32,256]{2,1,0:T(8,128)S(1)} collective-permute-done((f32[8,32,256]{2,1,0:T(8,128)S(1)}, f32[8,32,256]{2,1,0:T(8,128)S(1)}, u32[]{:S(2)}, u32[]{:S(2)}) %collective-permute-start.3) | collective-permute-done | bytes 262176 | tf_op jit(solution)/shard_map/ppermute | solution.py:115
  56.8 0.6 gather_fusion
  57.4 0.4 convolution_bitcast_fusion
  57.9 1.2 add_divide_fusion
  59.2 0.7 copy-done.10
  59.9 0.3 maximum_subtract_fusion
  60.3 4.2 %scatter_fusion = f32[3,8,32,256]{3,2,1,0:T(8,128)S(1)} fusion(f32[3,8,32,256]{3,2,1,0:T(8,128)S(1)} %maximum_subtract_fusion, s32[48]{0:T(128)S(1)} %fusion.59, f32[48]{0:T(128)S(1)} %reshape.207), kind=kCustom, calls=%fused_computation.1 | custom fusion | flops 48 | bytes 1344 | tf_op jit(solution)/shard_map/scatter-add | solution.py:133
  64.5 3.3 %multiply_reduce_fusion = (f32[8,32,256]{2,1,0:T(8,128)S(1)}, f32[3,8,32,256]{3,2,1,0:T(8,128)}, f32[3,8,32,256]{3,2,1,0:T(8,128)}) fusion(f32[3,8,32,256]{3,2,1,0:T(8,128)S(1)} %copy-done, f32[3,8,32,256]{3,2,1,0:T(8,128)S(1)} %copy-done.1, f32[8,32,256]{2,1,0:T(8,128)S(1)} %scatter_fusion.1, f32[3,8,32,256]{3,2,1,0:T(8,128)} %param.20, ...), kind=kLoop, calls=%fused_computation.15 | loop fusion | flops 3866624 | bytes 7340032 | tf_op jit(solution)/shard_map/reduce_sum | solution.py:142
  67.8 0.5 fusion.23
  68.3 1.1 copy.22
  69.4 55.1 %reduce-scatter.2.cloned.1.call-done = f32[1,32,256]{2,1,0:T(8,128)} async-done(((f32[16,32,256]{2,1,0:T(8,128)}), f32[1,32,256]{2,1,0:T(8,128)}) %reduce-scatter.2.cloned.1.call-update) | async-done | bytes 32784 | tf_op jit(solution)/shard_map/reduce_scatter | solution.py:146
  124.6 1.0 convolution_bitcast_fusion.2
  125.6 0.9 convolution_bitcast_fusion.1
  (98 shorter events, 1.6 us)
Async XLA Ops:
  7.2 117.4 %reduce-scatter.2.cloned.1.call-start = ((), (), s32[]{:S(2)}) async-start(), calls=%async_computation.1 | async-start | bytes 557056 | tf_op jit(solution)/shard_map/reduce_scatter | solution.py:146
  8.0 2.1 %copy-start.18 = (f32[1,32,256]{2,1,0:T(8,128)S(1)}, f32[1,32,256]{2,1,0:T(8,128)}, u32[]{:S(2)}) copy-start(f32[1,32,256]{2,1,0:T(8,128)} %param.22) | copy-start | bytes 98308
  8.7 10.0 %copy-start = (f32[3,8,32,256]{3,2,1,0:T(8,128)S(1)}, f32[3,8,32,256]{3,2,1,0:T(8,128)}, u32[]{:S(2)}) copy-start(f32[3,8,32,256]{3,2,1,0:T(8,128)} %param.14) | copy-start | bytes 2359300
  8.7 26.8 %collective-permute-start.4 = (f32[4,32,256]{2,1,0:T(8,128)}, f32[4,32,256]{2,1,0:T(8,128)}, u32[]{:S(2)}, u32[]{:S(2)}) collective-permute-start(f32[4,32,256]{2,1,0:T(8,128)} %pad_maximum_fusion.2), channel_id=1, source_target_pairs={{1,0},{2,1},{3,2},{4,3},{5,4},{6,5},{7,6},{8,7},{9,8},{10,9},{11,1... | collective-permute-start | bytes 393224 | tf_op jit(solution)/shard_map/ppermute | solution.py:18
  10.1 20.3 %collective-permute-start = (f32[1,32,256]{2,1,0:T(8,128)S(1)}, f32[1,32,256]{2,1,0:T(8,128)S(1)}, u32[]{:S(2)}, u32[]{:S(2)}) collective-permute-start(f32[1,32,256]{2,1,0:T(8,128)S(1)} %copy-done.18), channel_id=1, source_target_pairs={{0,15},{1,0},{2,1},{3,2},{4,3},{5,4},{6,5},{7,6},{8,7},{9,8},{10,9... | collective-permute-start | bytes 98312 | tf_op jit(solution)/shard_map/ppermute | solution.py:115
  18.7 1.3 copy-start.1
  22.9 0.7 copy-start.25
  22.9 0.7 copy-start.26
  24.0 0.7 copy-start.24
  25.8 0.9 copy-start.14
  26.7 0.9 copy-start.13
  30.4 5.9 %copy-start.17 = (f32[7,32,256]{2,1,0:T(8,128)S(1)}, f32[7,32,256]{2,1,0:T(8,128)}, u32[]{:S(2)}) copy-start(f32[7,32,256]{2,1,0:T(8,128)} %get-tuple-element.38) | copy-start | bytes 688132
  30.5 4.3 %collective-permute-start.1 = (f32[2,32,256]{2,1,0:T(8,128)S(1)}, f32[2,32,256]{2,1,0:T(8,128)S(1)}, u32[]{:S(2)}, u32[]{:S(2)}) collective-permute-start(f32[2,32,256]{2,1,0:T(8,128)S(1)} %pad_maximum_fusion.4), channel_id=1, source_target_pairs={{0,14},{1,15},{2,0},{3,1},{4,2},{5,3},{6,4},{7,5},{8,6},{9,7},{10,... | collective-permute-start | bytes 196616 | tf_op jit(solution)/shard_map/ppermute | solution.py:115
  34.8 1.6 %copy-start.12 = (f32[8,32,255]{2,1,0:T(8,128)S(1)}, f32[8,32,255]{2,1,0:T(8,128)}, u32[]{:S(2)}) copy-start(f32[8,32,255]{2,1,0:T(8,128)} %slice.274) | copy-start | bytes 783364
  34.8 1.6 %copy-start.11 = (f32[8,31,256]{2,1,0:T(8,128)S(1)}, f32[8,31,256]{2,1,0:T(8,128)}, u32[]{:S(2)}) copy-start(f32[8,31,256]{2,1,0:T(8,128)} %slice.273) | copy-start | bytes 761860
  34.8 7.1 %collective-permute-start.2 = (f32[4,32,256]{2,1,0:T(8,128)S(1)}, f32[4,32,256]{2,1,0:T(8,128)S(1)}, u32[]{:S(2)}, u32[]{:S(2)}) collective-permute-start(f32[4,32,256]{2,1,0:T(8,128)S(1)} %pad_maximum_fusion.1), channel_id=1, source_target_pairs={{0,12},{1,13},{2,14},{3,15},{4,0},{5,1},{6,2},{7,3},{8,4},{9,5},{1... | collective-permute-start | bytes 393224 | tf_op jit(solution)/shard_map/ppermute | solution.py:115
  36.4 1.2 copy-start.21
  37.7 5.1 %copy-start.2 = (f32[3,8,32,256]{3,2,1,0:T(8,128)}, f32[3,8,32,256]{3,2,1,0:T(8,128)S(1)}, u32[]{:S(2)}) copy-start(f32[3,8,32,256]{3,2,1,0:T(8,128)S(1)} %fusion) | copy-start | bytes 2359300
  37.8 1.2 copy-start.15
  37.8 1.3 copy-start.16
  39.1 1.1 copy-start.22
  40.3 3.7 %copy-start.3 = (f32[3,8,32,256]{3,2,1,0:T(8,128)}, f32[3,8,32,256]{3,2,1,0:T(8,128)S(1)}, u32[]{:S(2)}) copy-start(f32[3,8,32,256]{3,2,1,0:T(8,128)S(1)} %fusion.1) | copy-start | bytes 2359300
  40.4 1.6 %copy-start.23 = (f32[32,32,256]{2,1,0:T(8,128)S(1)}, f32[32,32,256]{2,1,0:T(8,128)}, u32[]{:S(2)}) copy-start(f32[32,32,256]{2,1,0:T(8,128)} %constant_dynamic-update-slice_fusion.7) | copy-start | bytes 3145732
  40.4 2.4 %collective-permute-start.5 = (f32[4,32,256]{2,1,0:T(8,128)S(1)}, f32[4,32,256]{2,1,0:T(8,128)S(1)}, u32[]{:S(2)}, u32[]{:S(2)}) collective-permute-start(f32[4,32,256]{2,1,0:T(8,128)S(1)} %pad_maximum_fusion.3), channel_id=1, source_target_pairs={{0,1},{1,2},{2,3},{3,4},{4,5},{5,6},{6,7},{7,8},{8,9},{9,10},{10,1... | collective-permute-start | bytes 393224 | tf_op jit(solution)/shard_map/ppermute | solution.py:18
  42.0 14.7 %collective-permute-start.3 = (f32[8,32,256]{2,1,0:T(8,128)S(1)}, f32[8,32,256]{2,1,0:T(8,128)S(1)}, u32[]{:S(2)}, u32[]{:S(2)}) collective-permute-start(f32[8,32,256]{2,1,0:T(8,128)S(1)} %pad_maximum_fusion), channel_id=1, source_target_pairs={{0,8},{1,9},{2,10},{3,11},{4,12},{5,13},{6,14},{7,15},{8,0},{9,1},... | collective-permute-start | bytes 786440 | tf_op jit(solution)/shard_map/ppermute | solution.py:115
  57.4 2.4 %copy-start.20 = (f32[3,8,32,256]{3,2,1,0:T(8,128)S(1)}, f32[3,8,32,256]{3,2,1,0:T(8,128)}, u32[]{:S(2)}) copy-start(f32[3,8,32,256]{3,2,1,0:T(8,128)} %param.17) | copy-start | bytes 2359300
  57.9 2.0 %copy-start.4 = (f32[1,8,32,256]{3,2,1,0:T(8,128)S(1)}, f32[1,8,32,256]{3,2,1,0:T(8,128)}, u32[]{:S(2)}) copy-start(f32[1,8,32,256]{3,2,1,0:T(8,128)} %get-tuple-element.17) | copy-start | bytes 786436
  57.9 2.0 %copy-start.5 = (f32[1,8,32,256]{3,2,1,0:T(8,128)S(1)}, f32[1,8,32,256]{3,2,1,0:T(8,128)}, u32[]{:S(2)}) copy-start(f32[1,8,32,256]{3,2,1,0:T(8,128)} %get-tuple-element.18) | copy-start | bytes 786436
  57.9 2.0 %copy-start.6 = (f32[1,8,32,256]{3,2,1,0:T(8,128)S(1)}, f32[1,8,32,256]{3,2,1,0:T(8,128)}, u32[]{:S(2)}) copy-start(f32[1,8,32,256]{3,2,1,0:T(8,128)} %get-tuple-element.19) | copy-start | bytes 786436
  57.9 2.0 %copy-start.19 = (f32[3,8,32,256]{3,2,1,0:T(8,128)S(1)}, f32[3,8,32,256]{3,2,1,0:T(8,128)}, u32[]{:S(2)}) copy-start(f32[3,8,32,256]{3,2,1,0:T(8,128)} %param.16) | copy-start | bytes 2359300
  59.2 0.7 copy-start.10
  60.2 4.3 %copy-start.7 = (f32[1,8,32,256]{3,2,1,0:T(8,128)S(1)}, f32[1,8,32,256]{3,2,1,0:T(8,128)}, u32[]{:S(2)}) copy-start(f32[1,8,32,256]{3,2,1,0:T(8,128)} %get-tuple-element.25) | copy-start | bytes 786436
  60.2 4.3 %copy-start.8 = (f32[1,8,32,256]{3,2,1,0:T(8,128)S(1)}, f32[1,8,32,256]{3,2,1,0:T(8,128)}, u32[]{:S(2)}) copy-start(f32[1,8,32,256]{3,2,1,0:T(8,128)} %get-tuple-element.26) | copy-start | bytes 786436
  60.3 4.3 %copy-start.9 = (f32[1,8,32,256]{3,2,1,0:T(8,128)S(1)}, f32[1,8,32,256]{3,2,1,0:T(8,128)}, u32[]{:S(2)}) copy-start(f32[1,8,32,256]{3,2,1,0:T(8,128)} %get-tuple-element.27) | copy-start | bytes 786436
Sparse Core Ops, SparseCore 0:
  69.6 54.9 reduce-scatter.1
